TPU v7x, 512 devices: a whole 4x4x16 slice. The times are simulated.
512 devices in a mesh: dp: 8 (over x, y_hi), expert: 64 (over y_lo, z, core).
Axes of the slice: x: 4, y: 4 (y_hi: 2, y_lo: 2; y = y_hi * 2 + y_lo), z: 16, core: 2. Of those that a mesh axis runs over, the one named last changes fastest.
Arguments:
- tokens: bfloat16 [65536, 2048], P(('dp', 'expert')), may hold values from -6 to 6
- out_grad: bfloat16 [65536, 2048], P(('dp', 'expert')), may hold values from -6 to 6
- combine: float32 [65536, 2], P(('dp', 'expert')), may hold values from 0.1 to 1
- expert_ids: int32 [65536, 2], P(('dp', 'expert')), may hold values from 0 to 63, all different within a row; in each aligned block of 128 rows (0 to 127, 128 to 255, ...) at most 5 rows name the same one
- gate_weight: bfloat16 [64, 2048, 768], P('expert', 'dp'), may hold values from -0.125 to 0.125
- up_weight: bfloat16 [64, 2048, 768], P('expert', 'dp'), may hold values from -0.125 to 0.125
- down_weight: bfloat16 [64, 2048, 768], P('expert', 'dp'), may hold values from -0.21875 to 0.21875
Outputs:
- token_grad: bfloat16 [65536, 2048], P(('dp', 'expert'))
- down_grad: bfloat16 [64, 2048, 768], P('expert', 'dp')
Inputs may be any that keep to these rules, and one draw needn't show every extreme that they name: `expert_ids`: each row names 2 different experts. Among the 128 rows of one device no expert is named more than 5 times, a bound that some block reaches.
All inputs are finite; a program needn't handle non-finite values.
Results may differ from a plain program's by a relative error of at most 0.012.
Values may be sent and summed in bfloat16 or wider, within the bound.
No kernel may reach another device: no remote copies, remote signals or barrier semaphores. Data moves between devices by JAX's collectives and lax.ppermute only.
A program may use at most 64 MiB of HBM per device.

v0:
```python
import jax
import jax.numpy as jnp
from jax import lax
from jax.sharding import PartitionSpec as P

TOP = 2


def forward_portion(rows_in, w_gate, w_up):
    gate_pre = jnp.dot(rows_in, w_gate, preferred_element_type=jnp.float32)
    up_pre = jnp.dot(rows_in, w_up, preferred_element_type=jnp.float32)
    sigmoid_gate = jax.nn.sigmoid(gate_pre)
    silu_gate = gate_pre * sigmoid_gate
    hidden = (silu_gate * up_pre).astype(jnp.bfloat16)
    return (gate_pre, up_pre, sigmoid_gate, silu_gate, hidden)


def body(tokens, out_grad, combine, expert_ids, gate_weight, up_weight, down_weight):
    token_rows = tokens.shape[0]
    embedding_width = tokens.shape[1]
    expert_count = lax.axis_size("expert")
    capacity = token_rows * TOP * 5 // (4 * expert_count)
    positions = expert_count * capacity
    flattened_identifiers = expert_ids.reshape(-1)
    onehot = (
        flattened_identifiers[:, None] == jnp.arange(expert_count, dtype=jnp.int32)[None, :]
    ).astype(jnp.int32)
    earlier = jnp.cumsum(onehot, axis=0) - onehot
    slot_index = jnp.sum(earlier * onehot, axis=1)
    target = flattened_identifiers * capacity + slot_index
    matches = target[None, :] == jnp.arange(positions, dtype=jnp.int32)[:, None]
    picker = jnp.sum(
        matches.reshape(positions, token_rows, TOP).astype(jnp.float32), axis=2
    ).astype(jnp.bfloat16)
    slot_weight = jnp.sum(
        jnp.where(matches, combine.reshape(-1)[None, :], jnp.float32(0.0)), axis=1
    )
    row_send = jnp.dot(picker, tokens, preferred_element_type=jnp.float32).astype(jnp.bfloat16)
    row_send = row_send.reshape(expert_count, capacity, embedding_width)
    picked_grad = jnp.dot(picker, out_grad, preferred_element_type=jnp.float32)
    grad_send = (slot_weight[:, None] * picked_grad).astype(jnp.bfloat16)
    grad_send = grad_send.reshape(expert_count, capacity, embedding_width)
    gathered = (
        lax.all_gather(gate_weight, "dp", axis=1, tiled=True),
        lax.all_gather(up_weight, "dp", axis=1, tiled=True),
        lax.all_gather(down_weight, "dp", axis=1, tiled=True),
    )
    w_gate = gathered[0][0]
    w_up = gathered[1][0]
    w_down = gathered[2][0]
    rows_in, grads_in = (
        lax.all_to_all(row_send, "expert", split_axis=0, concat_axis=0, tiled=True),
        lax.all_to_all(grad_send, "expert", split_axis=0, concat_axis=0, tiled=True),
    )
    rows_in = rows_in.reshape(positions, embedding_width)
    grads_in = grads_in.reshape(positions, embedding_width)
    gate_pre, up_pre, sigmoid_gate, silu_gate, hidden = forward_portion(rows_in, w_gate, w_up)
    hidden_grad = jnp.dot(grads_in, w_down, preferred_element_type=jnp.float32)
    gate_grad = (
        hidden_grad * up_pre * sigmoid_gate * (1.0 + gate_pre * (1.0 - sigmoid_gate))
    ).astype(jnp.bfloat16)
    up_grad = (hidden_grad * silu_gate).astype(jnp.bfloat16)
    contract_hidden = (((1,), (1,)), ((), ()))
    row_grad = (
        lax.dot_general(gate_grad, w_gate, contract_hidden, preferred_element_type=jnp.float32)
        + lax.dot_general(up_grad, w_up, contract_hidden, preferred_element_type=jnp.float32)
    ).astype(jnp.bfloat16)
    back_rows = lax.all_to_all(
        row_grad.reshape(expert_count, capacity, embedding_width),
        "expert",
        split_axis=0,
        concat_axis=0,
        tiled=True,
    )
    token_grad = lax.dot_general(
        picker,
        back_rows.reshape(positions, embedding_width),
        (((0,), (0,)), ((), ())),
        preferred_element_type=jnp.float32,
    ).astype(jnp.bfloat16)
    down_grad = lax.psum_scatter(
        lax.dot_general(
            grads_in, hidden, (((0,), (0,)), ((), ())), preferred_element_type=jnp.float32
        ).astype(jnp.bfloat16),
        "dp",
        scatter_dimension=0,
        tiled=True,
    )
    return (token_grad, down_grad[None])


def solution(mesh):
    placed = (
        P(("dp", "expert"), None),
        P(("dp", "expert"), None),
        P(("dp", "expert"), None),
        P(("dp", "expert"), None),
        P("expert", "dp", None),
        P("expert", "dp", None),
        P("expert", "dp", None),
    )
    return jax.shard_map(
        body,
        mesh=mesh,
        in_specs=placed,
        out_specs=(P(("dp", "expert"), None), P("expert", "dp", None)),
        check_vma=False,
    )
```

profile of v0, /device:TPU:6, one launch (start us, length us, event | category | flops | bytes accessed | tf_op | source)
XLA Modules:
  0.0 399.3 jit_solution(16385939312701261271)
XLA Ops:
  7.2 0.0 copy-start
  7.2 0.0 all-gather.8.cloned.1.call-start
  7.2 0.7 all-gather.8.cloned.1.call-update
  7.9 0.8 copy.23
  8.7 0.1 eq.49
  8.8 0.1 eq.45
  9.0 0.6 reduce-window.6
  9.6 0.2 slice_reduce_fusion
  9.8 0.1 fusion.23
  9.9 0.1 reduce_sum.30
  10.1 0.1 copy.26
  10.2 0.8 copy.27
  11.0 0.1 broadcast_in_dim.21
  11.1 0.7 multiply_add_fusion.1
  11.9 0.1 select_reduce_fusion
  12.0 0.0 copy-done
  12.0 0.5 fusion.16
  12.5 1.6 reshape.61
  14.1 0.0 copy-start.2
  14.1 17.2 %all-to-all-start = ((bf16[64,5,2048]{2,1,0:T(8,128)(2,1)}), bf16[64,5,2048]{2,1,0:T(8,128)(2,1)S(1)}, u32[]{:S(2)}, u32[]{:S(2)}) async-start(bf16[64,5,2048]{2,1,0:T(8,128)(2,1)} %reshape.61), calls=%async_computation | async-start | bytes 4194304 | tf_op jit(solution)/shard_map/all_to_all | solution.py:53
  31.4 0.0 all-gather.6.cloned.1.call-start
  31.4 0.7 all-gather.6.cloned.1.call-update
  32.1 0.0 copy-done.2
  32.1 1.6 convolution_convert_fusion.1
  33.7 3.4 reshape.63
  37.1 90.9 %all-to-all-done = bf16[64,5,2048]{2,1,0:T(8,128)(2,1)S(1)} async-done(((bf16[64,5,2048]{2,1,0:T(8,128)(2,1)}), bf16[64,5,2048]{2,1,0:T(8,128)(2,1)S(1)}, u32[]{:S(2)}, u32[]{:S(2)}) %all-to-all-start) | async-done | bytes 1310752 | tf_op jit(solution)/shard_map/all_to_all | solution.py:53
  128.1 8.6 %all-to-all-start.1 = ((bf16[64,5,2048]{2,1,0:T(8,128)(2,1)}), bf16[64,5,2048]{2,1,0:T(8,128)(2,1)}, u32[]{:S(2)}, u32[]{:S(2)}) async-start(bf16[64,5,2048]{2,1,0:T(8,128)(2,1)} %reshape.63), calls=%async_computation.1 | async-start | bytes 4194304 | tf_op jit(solution)/shard_map/all_to_all | solution.py:52
  136.7 0.0 all-gather.4.cloned.1.call-start
  136.7 0.7 all-gather.4.cloned.1.call-update
  137.4 0.2 reduce-scatter.2.cloned.1.call-start
  137.6 1.4 reshape.62
  139.1 94.1 %all-to-all-done.1 = bf16[64,5,2048]{2,1,0:T(8,128)(2,1)} async-done(((bf16[64,5,2048]{2,1,0:T(8,128)(2,1)}), bf16[64,5,2048]{2,1,0:T(8,128)(2,1)}, u32[]{:S(2)}, u32[]{:S(2)}) %all-to-all-start.1) | async-done | bytes 1310752 | tf_op jit(solution)/shard_map/all_to_all | solution.py:52
  233.2 2.6 reshape.64
  235.8 0.0 all-gather.8.cloned.1.call-done
  235.8 4.0 %fusion.2 = f32[320,768]{1,0:T(8,128)} fusion(bf16[320,2048]{1,0:T(8,128)(2,1)S(1)} %reshape.64, bf16[1,2048,768]{2,1,0:T(8,128)(2,1)} %all-gather.8.cloned.1.call-done), kind=kOutput, calls=%fused_computation.3 | convolution fusion | flops 1006632960 | bytes 5439488 | tf_op jit(solution)/shard_map/dot_general | solution.py:10
  239.8 0.0 copy-start.1
  239.8 0.0 all-gather.6.cloned.1.call-done
  239.8 0.0 copy-start.5
  239.8 3.4 fusion.6
  243.2 0.0 copy-start.7
  243.2 1.0 copy-done.7
  244.2 0.0 copy-done.1
  244.2 0.0 copy-done.5
  244.2 3.7 convolution_convert_fusion
  247.9 0.0 reduce-scatter.2.cloned.1.call-update
  247.9 0.0 copy-start.6
  247.9 21.4 %all-gather.4.cloned.1.call-done = bf16[1,2048,768]{2,1,0:T(8,128)(2,1)} async-done(((bf16[1,256,768]{2,1,0:T(8,128)(2,1)}), bf16[1,2048,768]{2,1,0:T(8,128)(2,1)}) %all-gather.4.cloned.1.call-update) | async-done | bytes 3145744 | tf_op jit(solution)/shard_map/all_gather | solution.py:46
  269.3 0.0 copy-start.3
  269.3 0.0 copy-start.8
  269.3 3.2 fusion.8
  272.5 0.0 copy-done.6
  272.5 0.0 copy-done.3
  272.5 0.0 copy-done.8
  272.5 0.0 copy-start.4
  272.6 1.3 fusion
  273.9 0.5 copy-done.4
  274.4 2.3 fusion.13
  276.7 2.4 reshape.65
  279.1 109.8 %all_to_all.15 = bf16[64,5,2048]{2,1,0:T(8,128)(2,1)} all-to-all(bf16[64,5,2048]{2,1,0:T(8,128)(2,1)S(1)} %reshape.65), channel_id=1, replica_groups=mesh['dp'=8,'expert'=64] {'expert'}, dimensions={0} | all-to-all | bytes 2621440 | tf_op jit(solution)/shard_map/all_to_all | solution.py:68
  388.9 2.6 reshape.66
  391.5 1.3 convolution_convert_fusion.2
  392.8 0.0 reduce-scatter.2.cloned.1.call-done
  (5 shorter events, 0.1 us)
Async XLA Ops:
  7.2 4.8 %copy-start = (bf16[128,2048]{1,0:T(8,128)(2,1)S(1)}, bf16[128,2048]{1,0:T(8,128)(2,1)}, u32[]{:S(2)}) copy-start(bf16[128,2048]{1,0:T(8,128)(2,1)} %param.8) | copy-start | bytes 1572868
  7.2 228.6 %all-gather.8.cloned.1.call-start = ((), (), s32[]{:S(2)}) async-start(), calls=%async_computation.6 | async-start | bytes 3538944 | tf_op jit(solution)/shard_map/all_gather | solution.py:44
  14.1 18.0 %copy-start.2 = (bf16[128,2048]{1,0:T(8,128)(2,1)S(1)}, bf16[128,2048]{1,0:T(8,128)(2,1)}, u32[]{:S(2)}) copy-start(bf16[128,2048]{1,0:T(8,128)(2,1)} %param.7) | copy-start | bytes 1572868
  14.1 113.9 %all-to-all-start = ((bf16[64,5,2048]{2,1,0:T(8,128)(2,1)}), bf16[64,5,2048]{2,1,0:T(8,128)(2,1)S(1)}, u32[]{:S(2)}, u32[]{:S(2)}) async-start(bf16[64,5,2048]{2,1,0:T(8,128)(2,1)} %reshape.61), calls=%async_computation | async-start | bytes 4194304 | tf_op jit(solution)/shard_map/all_to_all | solution.py:53
  31.4 208.4 %all-gather.6.cloned.1.call-start = ((), (), s32[]{:S(2)}) async-start(), calls=%async_computation.5 | async-start | bytes 3538944 | tf_op jit(solution)/shard_map/all_gather | solution.py:45
  128.1 105.1 %all-to-all-start.1 = ((bf16[64,5,2048]{2,1,0:T(8,128)(2,1)}), bf16[64,5,2048]{2,1,0:T(8,128)(2,1)}, u32[]{:S(2)}, u32[]{:S(2)}) async-start(bf16[64,5,2048]{2,1,0:T(8,128)(2,1)} %reshape.63), calls=%async_computation.1 | async-start | bytes 4194304 | tf_op jit(solution)/shard_map/all_to_all | solution.py:52
  136.7 132.6 %all-gather.4.cloned.1.call-start = ((), (), s32[]{:S(2)}) async-start(), calls=%async_computation.4 | async-start | bytes 3538944 | tf_op jit(solution)/shard_map/all_gather | solution.py:46
  137.4 255.4 %reduce-scatter.2.cloned.1.call-start = ((), (), s32[]{:S(2)}) async-start(), calls=%async_computation.7 | async-start | bytes 3538944 | tf_op jit(solution)/shard_map/reduce_scatter | solution.py:81
  239.8 4.4 %copy-start.1 = (bf16[320,2048]{1,0:T(8,128)(2,1)S(1)}, bf16[320,2048]{1,0:T(8,128)(2,1)}, u32[]{:S(2)}) copy-start(bf16[320,2048]{1,0:T(8,128)(2,1)} %reshape.62) | copy-start | bytes 3932164
  239.8 4.4 %copy-start.5 = (f32[320,768]{1,0:T(8,128)S(1)}, f32[320,768]{1,0:T(8,128)}, u32[]{:S(2)}) copy-start(f32[320,768]{1,0:T(8,128)} %fusion.2) | copy-start | bytes 2949124
  243.2 1.0 copy-start.7
  247.9 24.6 %copy-start.6 = (f32[320,768]{1,0:T(8,128)S(1)}, f32[320,768]{1,0:T(8,128)}, u32[]{:S(2)}) copy-start(f32[320,768]{1,0:T(8,128)} %fusion.2) | copy-start | bytes 2949124
  269.3 3.2 copy-start.3
  269.3 3.2 copy-start.8
  272.5 1.9 copy-start.4
Sparse Core Ops, SparseCore 0:
  11.2 88.9 all-gather.7
  103.3 82.1 all-gather.5
  188.7 80.5 all-gather.3
  274.5 100.6 reduce-scatter.1
where the time goes:
time: 402 us; the launch traced here: 399 us
  waiting for transfers between devices  209 us (52%)
  blocking collectives  110 us (27%)
  starting transfers between devices  26.2 us (7%)
  matrix products  21.2 us (5%)
  local copies, waits for them, and re-layouts  17.9 us (4%)
  between operations  14 us (3%)
    all_to_all x1, blocking collectives, body(): lax.all_to_all(row_grad.reshape(expert_count, capacity, embedding_width),...  110 us
    all_to_all x1, waiting for transfers between devices, body(): lax.all_to_all(row_send, 'expert', split_axis=0, concat_axis=0, tiled=True)  94.1 us
    all_to_all x1, waiting for transfers between devices, body(): lax.all_to_all(grad_send, 'expert', split_axis=0, concat_axis=0, tiled=True)  90.9 us
    all_gather x1, waiting for transfers between devices, body(): lax.all_gather(down_weight, 'dp', axis=1, tiled=True)  21.4 us
    all_to_all x1, starting transfers between devices, body(): lax.all_to_all(grad_send, 'expert', split_axis=0, concat_axis=0, tiled=True)  17.2 us
    all_to_all x1, starting transfers between devices, body(): lax.all_to_all(row_send, 'expert', split_axis=0, concat_axis=0, tiled=True)  8.58 us
  transfers between devices with their start and end apart: 6, of which 3 were waited for; matrix products, arithmetic and copies ran while one was open for 10% of the time, Pallas kernels for 0%

commit v1 on v0

v1 whole, which is shorter than its diff:
```python
import jax
import jax.numpy as jnp
from jax import lax
from jax.sharding import Mesh
from jax.sharding import PartitionSpec as P

TOP = 2
CAP = 5
SUB = ("ylo", "z", "core")
ROWS = ("dp",) + SUB


def local_then_z(x, kinds):
    x = lax.all_to_all(x, "core", 3, 3, tiled=True)
    x = lax.all_to_all(x, "ylo", 1, 1, tiled=True)
    return [lax.all_to_all(x[k], "z", 1, 1, tiled=True) for k in range(kinds)]


def z_then_local(x):
    x = lax.all_to_all(x, "z", 1, 1, tiled=True)
    x = lax.all_to_all(x, "ylo", 0, 0, tiled=True)
    return lax.all_to_all(x, "core", 2, 2, tiled=True)


def body(tokens, out_grad, combine, expert_ids, gate_weight, up_weight, down_weight):
    token_rows = tokens.shape[0]
    width = tokens.shape[1]
    n_ylo, n_z, n_core = (lax.axis_size(a) for a in SUB)
    expert_count = n_ylo * n_z * n_core
    capacity = CAP
    positions = expert_count * capacity
    w_gate = lax.all_gather(gate_weight, "dp", axis=1, tiled=True)[0]
    w_up = lax.all_gather(up_weight, "dp", axis=1, tiled=True)[0]
    w_down = lax.all_gather(down_weight, "dp", axis=1, tiled=True)[0]
    flat_ids = expert_ids.reshape(-1)
    onehot = (flat_ids[:, None] == jnp.arange(expert_count, dtype=jnp.int32)[None, :]).astype(jnp.int32)
    earlier = jnp.cumsum(onehot, axis=0) - onehot
    slot_index = jnp.sum(earlier * onehot, axis=1)
    target = flat_ids * capacity + slot_index
    matches = target[None, :] == jnp.arange(positions, dtype=jnp.int32)[:, None]
    picker = jnp.sum(
        matches.reshape(positions, token_rows, TOP).astype(jnp.float32), axis=2
    ).astype(jnp.bfloat16)
    slot_weight = jnp.sum(jnp.where(matches, combine.reshape(-1)[None, :], jnp.float32(0.0)), axis=1)
    row_send = jnp.dot(picker, tokens, preferred_element_type=jnp.float32).astype(jnp.bfloat16)
    picked_grad = jnp.dot(picker, out_grad, preferred_element_type=jnp.float32)
    grad_send = (slot_weight[:, None] * picked_grad).astype(jnp.bfloat16)
    send = jnp.stack([row_send, grad_send]).reshape(2, n_ylo, n_z, n_core, capacity, width)
    rows_in, grads_in = local_then_z(send, 2)
    rows_in = rows_in.reshape(positions, width)
    grads_in = grads_in.reshape(positions, width)
    gate_pre = jnp.dot(rows_in, w_gate, preferred_element_type=jnp.float32)
    up_pre = jnp.dot(rows_in, w_up, preferred_element_type=jnp.float32)
    sigmoid_gate = jax.nn.sigmoid(gate_pre)
    silu_gate = gate_pre * sigmoid_gate
    hidden = (silu_gate * up_pre).astype(jnp.bfloat16)
    hidden_grad = jnp.dot(grads_in, w_down, preferred_element_type=jnp.float32)
    gate_grad = (
        hidden_grad * up_pre * sigmoid_gate * (1.0 + gate_pre * (1.0 - sigmoid_gate))
    ).astype(jnp.bfloat16)
    up_grad = (hidden_grad * silu_gate).astype(jnp.bfloat16)
    contract_hidden = (((1,), (1,)), ((), ()))
    row_grad = (
        lax.dot_general(gate_grad, w_gate, contract_hidden, preferred_element_type=jnp.float32)
        + lax.dot_general(up_grad, w_up, contract_hidden, preferred_element_type=jnp.float32)
    ).astype(jnp.bfloat16)
    back_rows = z_then_local(row_grad.reshape(n_ylo, n_z, n_core, capacity, width))
    token_grad = lax.dot_general(
        picker,
        back_rows.reshape(positions, width),
        (((0,), (0,)), ((), ())),
        preferred_element_type=jnp.float32,
    ).astype(jnp.bfloat16)
    down_grad = lax.psum_scatter(
        lax.dot_general(
            grads_in, hidden, (((0,), (0,)), ((), ())), preferred_element_type=jnp.float32
        ).astype(jnp.bfloat16),
        "dp",
        scatter_dimension=0,
        tiled=True,
    )
    return (token_grad, down_grad[None])


def solution(mesh):
    n_dp, n_expert = mesh.devices.shape
    fine = Mesh(mesh.devices.reshape(n_dp, 2, n_expert // 4, 2), ("dp",) + SUB)
    rows = P(ROWS, None)
    weights = P(SUB, "dp", None)
    return jax.shard_map(
        body,
        mesh=fine,
        in_specs=(rows, rows, rows, rows, weights, weights, weights),
        out_specs=(rows, weights),
        check_vma=False,
    )
```

time: 402 us -> 379 us (0.943)
  waiting for transfers between devices: 209 us -> 142 us
  blocking collectives: 110 us -> 141 us
  local copies, waits for them, and re-layouts: 17.9 us -> 30.7 us
  starting transfers between devices: 26.2 us -> 18.9 us
    all_to_all x2, waiting for transfers between devices: 185 us -> 118 us  [local_then_z(): return [lax.all_to_all(x[k], 'z', 1, 1, tiled=True) for k in range(kinds)]]
    all_to_all x1 -> x5, blocking collectives: 110 us -> 141 us  [the longest x1 74 us: z_then_local(): x = lax.all_to_all(x, 'z', 1, 1, tiled=True)]
    another operation x1 -> x4, local copies, waits for them, and re-layouts: 0.01 us -> 7.56 us  [the longest x3 7.55 us: body(): jnp.stack([row_send, grad_send])]
    all_to_all x2, starting transfers between devices: 25.8 us -> 18.5 us  [local_then_z(): return [lax.all_to_all(x[k], 'z', 1, 1, tiled=True) for k in range(kinds)]]
    all_to_all x0 -> x6, local copies, waits for them, and re-layouts: none -> 5.92 us  [the longest x2 4 us: local_then_z(): return [lax.all_to_all(x[k], 'z', 1, 1, tiled=True) for k in range(kinds)]]
    reshape x6 -> x5, local copies, waits for them, and re-layouts: 14 us -> 8.17 us  [the longest x2 3.91 us: body(): row_grad.reshape(n_ylo, n_z, n_core, capacity, width)]
    squeeze x0 -> x3, local copies, waits for them, and re-layouts: none -> 5.1 us  [local_then_z(): return [lax.all_to_all(x[k], 'z', 1, 1, tiled=True) for k in range(kinds)]]
  transfers between devices with their start and end apart: 6 -> 6, of which waited for: 3 -> 3; matrix products, arithmetic and copies ran while one was open for 10% -> 15% of each run, Pallas kernels for 0% -> 0%
where the time goes in v1:
time: 379 us; the launch traced here: 376 us
  waiting for transfers between devices  142 us (37%)
  blocking collectives  141 us (37%)
  local copies, waits for them, and re-layouts  30.7 us (8%)
  matrix products  24.3 us (6%)
  starting transfers between devices  18.9 us (5%)
  between operations  14 us (4%)
  other arithmetic  4.2 us (1%)
    all_to_all x2, waiting for transfers between devices, local_then_z(): return [lax.all_to_all(x[k], 'z', 1, 1, tiled=True) for k in range(kinds)]  118 us
    all_to_all x1, blocking collectives, z_then_local(): x = lax.all_to_all(x, 'z', 1, 1, tiled=True)  74 us
    all_to_all x1, blocking collectives, local_then_z(): x = lax.all_to_all(x, 'ylo', 1, 1, tiled=True)  39.7 us
    all_gather x1, waiting for transfers between devices, body(): w_down = lax.all_gather(down_weight, 'dp', axis=1, tiled=True)[0]  22.3 us
    all_to_all x2, starting transfers between devices, local_then_z(): return [lax.all_to_all(x[k], 'z', 1, 1, tiled=True) for k in range(kinds)]  18.5 us
    all_to_all x1, blocking collectives, z_then_local(): x = lax.all_to_all(x, 'ylo', 0, 0, tiled=True)  17 us
  transfers between devices with their start and end apart: 6, of which 3 were waited for; matrix products, arithmetic and copies ran while one was open for 15% of the time, Pallas kernels for 0%

profile of v1, /device:TPU:6, one launch (start us, length us, event | category | flops | bytes accessed | tf_op | source)
XLA Modules:
  0.0 375.6 jit_solution(1346013559021178343)
XLA Ops:
  7.2 0.0 copy-start
  7.2 0.0 all-gather.8.cloned.1.call-start
  7.2 0.7 all-gather.8.cloned.1.call-update
  7.9 0.8 copy.49
  8.7 0.1 eq.45
  8.8 0.1 eq.49
  9.0 0.8 copy.53
  9.8 0.1 broadcast_in_dim.21
  9.9 0.6 reduce-window.6
  10.5 0.2 slice_reduce_fusion
  10.8 0.1 fusion.23
  10.9 0.1 reduce_sum.30
  11.0 0.1 copy.52
  11.1 0.7 multiply_add_fusion.1
  11.9 0.1 select_reduce_fusion
  12.0 1.6 fusion.16
  13.6 2.4 stack.10
  16.0 0.0 copy-done.5
  16.0 1.6 convolution_convert_fusion.1
  17.6 3.4 stack.9
  21.0 2.5 pad_maximum_fusion
  23.5 1.7 copy.54
  25.3 5.8 %all_to_all.35 = bf16[2,2,16,2,5,2048]{5,2,4,1,0,3:T(8,128)(2,1)S(1)} all-to-all(bf16[2,2,16,2,5,2048]{5,2,4,1,0,3:T(8,128)(2,1)S(1)} %copy.54), channel_id=1, replica_groups=mesh['dp'=8,'ylo'=2,'z'=16,'core'=2] {'core'}, dimensions={3} | all-to-all | bytes 5242880 | tf_op jit(solution)/shard_map/all_to_all | solution.py:14
  31.1 0.3 copy.55
  31.5 39.7 %all_to_all.36 = bf16[2,2,16,2,5,2048]{5,2,4,3,0,1:T(8,128)(2,1)S(1)} all-to-all(bf16[2,2,16,2,5,2048]{5,2,4,3,0,1:T(8,128)(2,1)S(1)} %copy.55), channel_id=1, replica_groups=mesh['dp'=8,'ylo'=2,'z'=16,'core'=2] {'ylo'}, dimensions={1} | all-to-all | bytes 5242880 | tf_op jit(solution)/shard_map/all_to_all | solution.py:15
  71.1 0.3 slice_bitcast_fusion.1
  71.4 2.4 copy.58
  73.8 12.3 %all-to-all-start.3 = ((bf16[2,16,2,5,2048]{4,2,3,0,1:T(2,128)(2,1)}), bf16[2,16,2,5,2048]{4,2,3,0,1:T(2,128)(2,1)S(1)}, u32[]{:S(2)}, u32[]{:S(2)}) async-start(bf16[2,16,2,5,2048]{4,2,3,0,1:T(2,128)(2,1)} %copy.58), calls=%async_computation.3 | async-start | bytes 2621440 | tf_op jit(solution)/shard_map/all_to_all | solution.py:16
  86.1 0.0 all-gather.6.cloned.1.call-start
  86.2 0.7 all-gather.6.cloned.1.call-update
  86.9 2.4 copy.56
  89.3 59.1 %all-to-all-done.3 = bf16[2,16,2,5,2048]{4,2,3,0,1:T(2,128)(2,1)S(1)} async-done(((bf16[2,16,2,5,2048]{4,2,3,0,1:T(2,128)(2,1)}), bf16[2,16,2,5,2048]{4,2,3,0,1:T(2,128)(2,1)S(1)}, u32[]{:S(2)}, u32[]{:S(2)}) %all-to-all-start.3) | async-done | bytes 1310752 | tf_op jit(solution)/shard_map/all_to_all | solution.py:16
  148.4 6.2 %all-to-all-start.2 = ((bf16[2,16,2,5,2048]{4,2,3,0,1:T(2,128)(2,1)}), bf16[2,16,2,5,2048]{4,2,3,0,1:T(2,128)(2,1)}, u32[]{:S(2)}, u32[]{:S(2)}) async-start(bf16[2,16,2,5,2048]{4,2,3,0,1:T(2,128)(2,1)} %copy.56), calls=%async_computation.2 | async-start | bytes 2621440 | tf_op jit(solution)/shard_map/all_to_all | solution.py:16
  154.6 0.0 all-gather.4.cloned.1.call-start
  154.6 0.7 all-gather.4.cloned.1.call-update
  155.3 0.0 copy-done.2
  155.3 0.2 reduce-scatter.2.cloned.1.call-start
  155.6 2.0 copy.59
  157.6 1.4 reshape.61
  159.0 58.9 %all-to-all-done.2 = bf16[2,16,2,5,2048]{4,2,3,0,1:T(2,128)(2,1)} async-done(((bf16[2,16,2,5,2048]{4,2,3,0,1:T(2,128)(2,1)}), bf16[2,16,2,5,2048]{4,2,3,0,1:T(2,128)(2,1)}, u32[]{:S(2)}, u32[]{:S(2)}) %all-to-all-start.2) | async-done | bytes 1310752 | tf_op jit(solution)/shard_map/all_to_all | solution.py:16
  217.9 2.0 copy.57
  219.9 1.4 reshape.60
  221.3 4.6 %fusion.2 = f32[320,768]{1,0:T(8,128)} fusion(bf16[320,2048]{1,0:T(8,128)(2,1)} %reshape.61, bf16[1,2048,768]{2,1,0:T(8,128)(2,1)} %all-gather.8.cloned.1.call-done), kind=kOutput, calls=%fused_computation.4 | convolution fusion | flops 1006632960 | bytes 5439488 | tf_op jit(solution)/shard_map/dot_general | solution.py:52
  225.9 0.0 copy-done.4
  225.9 3.5 fusion.6
  229.5 0.9 copy-done.10
  230.4 3.6 convolution_convert_fusion
  234.0 0.0 reduce-scatter.2.cloned.1.call-update
  234.0 22.3 %all-gather.4.cloned.1.call-done = bf16[1,2048,768]{2,1,0:T(8,128)(2,1)} async-done(((bf16[1,256,768]{2,1,0:T(8,128)(2,1)}), bf16[1,2048,768]{2,1,0:T(8,128)(2,1)}) %all-gather.4.cloned.1.call-update) | async-done | bytes 3145744 | tf_op jit(solution)/shard_map/all_gather | solution.py:34
  256.3 3.2 fusion.8
  259.5 0.0 copy-done.9
  259.6 1.3 fusion
  260.9 0.5 copy-done.7
  261.5 2.3 fusion.13
  263.8 2.4 reshape.62
  266.1 1.5 copy.60
  267.7 74.0 %all_to_all.37 = bf16[2,16,2,5,2048]{4,2,3,0,1:T(2,128)(2,1)S(1)} all-to-all(bf16[2,16,2,5,2048]{4,2,3,0,1:T(2,128)(2,1)S(1)} %copy.60), channel_id=1, replica_groups=mesh['dp'=8,'ylo'=2,'z'=16,'core'=2] {'z'}, dimensions={1} | all-to-all | bytes 2621440 | tf_op jit(solution)/shard_map/all_to_all | solution.py:20
  341.6 0.7 copy.61
  342.4 17.0 %all_to_all.38 = bf16[2,16,2,5,2048]{4,1,3,2,0:T(8,128)(2,1)S(1)} all-to-all(bf16[2,16,2,5,2048]{4,1,3,2,0:T(8,128)(2,1)S(1)} %copy.61), channel_id=1, replica_groups=mesh['dp'=8,'ylo'=2,'z'=16,'core'=2] {'ylo'}, dimensions={0} | all-to-all | bytes 2621440 | tf_op jit(solution)/shard_map/all_to_all | solution.py:21
  359.4 0.1 copy.62
  359.5 4.8 %all_to_all.39 = bf16[2,16,2,5,2048]{4,1,3,0,2:T(8,128)(2,1)S(1)} all-to-all(bf16[2,16,2,5,2048]{4,1,3,0,2:T(8,128)(2,1)S(1)} %copy.62), channel_id=1, replica_groups=mesh['dp'=8,'ylo'=2,'z'=16,'core'=2] {'core'}, dimensions={2} | all-to-all | bytes 2621440 | tf_op jit(solution)/shard_map/all_to_all | solution.py:22
  364.3 0.7 copy.63
  365.1 1.4 reshape.63
  366.5 2.6 convolution_convert_fusion.2
  (25 shorter events, 0.1 us)
Async XLA Ops:
  7.2 4.8 %copy-start = (bf16[128,2048]{1,0:T(8,128)(2,1)S(1)}, bf16[128,2048]{1,0:T(8,128)(2,1)}, u32[]{:S(2)}) copy-start(bf16[128,2048]{1,0:T(8,128)(2,1)} %param.8) | copy-start | bytes 1572868
  7.2 214.1 %all-gather.8.cloned.1.call-start = ((), (), s32[]{:S(2)}) async-start(), calls=%async_computation.10 | async-start | bytes 3538944 | tf_op jit(solution)/shard_map/all_gather | solution.py:32
  13.6 2.4 copy-start.5
  73.8 74.5 %all-to-all-start.3 = ((bf16[2,16,2,5,2048]{4,2,3,0,1:T(2,128)(2,1)}), bf16[2,16,2,5,2048]{4,2,3,0,1:T(2,128)(2,1)S(1)}, u32[]{:S(2)}, u32[]{:S(2)}) async-start(bf16[2,16,2,5,2048]{4,2,3,0,1:T(2,128)(2,1)} %copy.58), calls=%async_computation.3 | async-start | bytes 2621440 | tf_op jit(solution)/shard_map/all_to_all | solution.py:16
  86.1 139.8 %all-gather.6.cloned.1.call-start = ((), (), s32[]{:S(2)}) async-start(), calls=%async_computation.9 | async-start | bytes 3538944 | tf_op jit(solution)/shard_map/all_gather | solution.py:33
  148.3 7.0 %copy-start.2 = (bf16[2,16,2,5,2048]{4,2,3,0,1:T(2,128)(2,1)}, bf16[2,16,2,5,2048]{4,2,3,0,1:T(2,128)(2,1)S(1)}, u32[]{:S(2)}) copy-start(bf16[2,16,2,5,2048]{4,2,3,0,1:T(2,128)(2,1)S(1)} %all-to-all-done.3) | copy-start | bytes 3932164
  148.4 69.5 %all-to-all-start.2 = ((bf16[2,16,2,5,2048]{4,2,3,0,1:T(2,128)(2,1)}), bf16[2,16,2,5,2048]{4,2,3,0,1:T(2,128)(2,1)}, u32[]{:S(2)}, u32[]{:S(2)}) async-start(bf16[2,16,2,5,2048]{4,2,3,0,1:T(2,128)(2,1)} %copy.56), calls=%async_computation.2 | async-start | bytes 2621440 | tf_op jit(solution)/shard_map/all_to_all | solution.py:16
  154.6 101.7 %all-gather.4.cloned.1.call-start = ((), (), s32[]{:S(2)}) async-start(), calls=%async_computation.8 | async-start | bytes 3538944 | tf_op jit(solution)/shard_map/all_gather | solution.py:34
  155.3 213.8 %reduce-scatter.2.cloned.1.call-start = ((), (), s32[]{:S(2)}) async-start(), calls=%async_computation.11 | async-start | bytes 3538944 | tf_op jit(solution)/shard_map/reduce_scatter | solution.py:74
  221.3 4.6 %copy-start.4 = (bf16[320,2048]{1,0:T(8,128)(2,1)S(1)}, bf16[320,2048]{1,0:T(8,128)(2,1)}, u32[]{:S(2)}) copy-start(bf16[320,2048]{1,0:T(8,128)(2,1)} %reshape.61) | copy-start | bytes 3932164
  225.9 4.5 %copy-start.3 = (bf16[320,2048]{1,0:T(8,128)(2,1)S(1)}, bf16[320,2048]{1,0:T(8,128)(2,1)}, u32[]{:S(2)}) copy-start(bf16[320,2048]{1,0:T(8,128)(2,1)} %reshape.60) | copy-start | bytes 3932164
  225.9 4.5 %copy-start.8 = (f32[320,768]{1,0:T(8,128)S(1)}, f32[320,768]{1,0:T(8,128)}, u32[]{:S(2)}) copy-start(f32[320,768]{1,0:T(8,128)} %fusion.2) | copy-start | bytes 2949124
  229.4 0.9 copy-start.10
  234.0 25.5 %copy-start.9 = (f32[320,768]{1,0:T(8,128)S(1)}, f32[320,768]{1,0:T(8,128)}, u32[]{:S(2)}) copy-start(f32[320,768]{1,0:T(8,128)} %fusion.2) | copy-start | bytes 2949124
  256.3 3.2 copy-start.6
  256.3 3.2 copy-start.11
  259.6 1.9 copy-start.7
  364.3 4.8 %copy-start.1 = (bf16[128,2048]{1,0:T(8,128)(2,1)S(1)}, bf16[128,2048]{1,0:T(8,128)(2,1)}, u32[]{:S(2)}) copy-start(bf16[128,2048]{1,0:T(8,128)(2,1)} %param.8) | copy-start | bytes 1572868
Sparse Core Ops, SparseCore 0:
  11.2 84.5 all-gather.7
  99.0 77.0 all-gather.5
  179.3 77.0 all-gather.3
  261.5 96.9 reduce-scatter.1

commit v2 on v1

--- a/solution.py
+++ b/solution.py
@@ -8,18 +8,26 @@
 CAP = 5
 SUB = ("ylo", "z", "core")
 ROWS = ("dp",) + SUB
+SWAP = [(0, 1), (1, 0)]
 
 
-def local_then_z(x, kinds):
-    x = lax.all_to_all(x, "core", 3, 3, tiled=True)
-    x = lax.all_to_all(x, "ylo", 1, 1, tiled=True)
-    return [lax.all_to_all(x[k], "z", 1, 1, tiled=True) for k in range(kinds)]
+def swap_half(x, axis_name, dim):
+    stay = lax.index_in_dim(x, 0, dim, keepdims=True)
+    go = lax.index_in_dim(x, 1, dim, keepdims=True)
+    got = lax.ppermute(go, axis_name, SWAP)
+    return jnp.concatenate([stay, got], dim)
 
 
-def z_then_local(x):
-    x = lax.all_to_all(x, "z", 1, 1, tiled=True)
-    x = lax.all_to_all(x, "ylo", 0, 0, tiled=True)
-    return lax.all_to_all(x, "core", 2, 2, tiled=True)
+def forward_move(x):
+    x = swap_half(x, "core", 0)
+    x = swap_half(x, "ylo", 1)
+    return lax.all_to_all(x, "z", 2, 2, tiled=True)
+
+
+def backward_move(x):
+    x = lax.all_to_all(x, "z", 2, 2, tiled=True)
+    x = swap_half(x, "ylo", 1)
+    return swap_half(x, "core", 0)
 
 
 def body(tokens, out_grad, combine, expert_ids, gate_weight, up_weight, down_weight):
@@ -29,14 +37,21 @@
     expert_count = n_ylo * n_z * n_core
     capacity = CAP
     positions = expert_count * capacity
-    w_gate = lax.all_gather(gate_weight, "dp", axis=1, tiled=True)[0]
-    w_up = lax.all_gather(up_weight, "dp", axis=1, tiled=True)[0]
-    w_down = lax.all_gather(down_weight, "dp", axis=1, tiled=True)[0]
+    stacked = lax.all_gather(
+        jnp.concatenate([gate_weight, up_weight, down_weight], 0), "dp", axis=1, tiled=True
+    )
+    w_gate, w_up, w_down = stacked[0], stacked[1], stacked[2]
     flat_ids = expert_ids.reshape(-1)
     onehot = (flat_ids[:, None] == jnp.arange(expert_count, dtype=jnp.int32)[None, :]).astype(jnp.int32)
     earlier = jnp.cumsum(onehot, axis=0) - onehot
     slot_index = jnp.sum(earlier * onehot, axis=1)
-    target = flat_ids * capacity + slot_index
+    my_core = lax.axis_index("core")
+    my_ylo = lax.axis_index("ylo")
+    e_core = flat_ids % n_core
+    e_z = (flat_ids // n_core) % n_z
+    e_ylo = flat_ids // (n_core * n_z)
+    rel = ((e_core ^ my_core) * n_ylo + (e_ylo ^ my_ylo)) * n_z + e_z
+    target = rel * capacity + slot_index
     matches = target[None, :] == jnp.arange(positions, dtype=jnp.int32)[:, None]
     picker = jnp.sum(
         matches.reshape(positions, token_rows, TOP).astype(jnp.float32), axis=2
@@ -45,10 +60,9 @@
     row_send = jnp.dot(picker, tokens, preferred_element_type=jnp.float32).astype(jnp.bfloat16)
     picked_grad = jnp.dot(picker, out_grad, preferred_element_type=jnp.float32)
     grad_send = (slot_weight[:, None] * picked_grad).astype(jnp.bfloat16)
-    send = jnp.stack([row_send, grad_send]).reshape(2, n_ylo, n_z, n_core, capacity, width)
-    rows_in, grads_in = local_then_z(send, 2)
-    rows_in = rows_in.reshape(positions, width)
-    grads_in = grads_in.reshape(positions, width)
+    block = (n_core, n_ylo, n_z, capacity, width)
+    rows_in = forward_move(row_send.reshape(block)).reshape(positions, width)
+    grads_in = forward_move(grad_send.reshape(block)).reshape(positions, width)
     gate_pre = jnp.dot(rows_in, w_gate, preferred_element_type=jnp.float32)
     up_pre = jnp.dot(rows_in, w_up, preferred_element_type=jnp.float32)
     sigmoid_gate = jax.nn.sigmoid(gate_pre)
@@ -64,7 +78,7 @@
         lax.dot_general(gate_grad, w_gate, contract_hidden, preferred_element_type=jnp.float32)
         + lax.dot_general(up_grad, w_up, contract_hidden, preferred_element_type=jnp.float32)
     ).astype(jnp.bfloat16)
-    back_rows = z_then_local(row_grad.reshape(n_ylo, n_z, n_core, capacity, width))
+    back_rows = backward_move(row_grad.reshape(block))
     token_grad = lax.dot_general(
         picker,
         back_rows.reshape(positions, width),

time: 379 us -> 328 us (0.87)
  blocking collectives: 141 us -> 0 us
  waiting for transfers between devices: 142 us -> 196 us
  starting transfers between devices: 18.9 us -> 52.7 us
  other arithmetic: 4.2 us -> 9.33 us
    all_to_all x5 -> x0, blocking collectives: 141 us -> none  [the longest x1 74 us: z_then_local(): x = lax.all_to_all(x, 'z', 1, 1, tiled=True)]
    ppermute x0 -> x6, waiting for transfers between devices: none -> 55.4 us  [swap_half(): got = lax.ppermute(go, axis_name, SWAP)]
    all_gather x3 -> x1, waiting for transfers between devices: 22.3 us -> 0.01 us  [body(): lax.all_gather(jnp.concatenate([gate_weight, up_weight, down_weight], 0),...]
    ppermute x0 -> x6, starting transfers between devices: none -> 18.2 us  [swap_half(): got = lax.ppermute(go, axis_name, SWAP)]
    all_to_all x2 -> x3, starting transfers between devices: 18.5 us -> 34.1 us  [the longest x2 27.9 us: forward_move(): return lax.all_to_all(x, 'z', 2, 2, tiled=True)]
    all_to_all x2 -> x3, waiting for transfers between devices: 118 us -> 133 us  [the longest x2 75.4 us: forward_move(): return lax.all_to_all(x, 'z', 2, 2, tiled=True)]
    slice x1 -> x16, local copies, waits for them, and re-layouts: 0.18 us -> 10.2 us  [the longest x10 6.14 us: swap_half(): go = lax.index_in_dim(x, 1, dim, keepdims=True)]
    concatenate x0 -> x5, other arithmetic: none -> 8.22 us  [the longest x4 5.74 us: swap_half(): return jnp.concatenate([stay, got], dim)]
  transfers between devices with their start and end apart: 6 -> 11, of which waited for: 3 -> 10; matrix products, arithmetic and copies ran while one was open for 15% -> 13% of each run, Pallas kernels for 0% -> 0%
where the time goes in v2:
time: 328 us; the launch traced here: 327 us
  waiting for transfers between devices  196 us (60%)
  starting transfers between devices  52.7 us (16%)
  local copies, waits for them, and re-layouts  32.8 us (10%)
  matrix products  21.2 us (6%)
  between operations  14.5 us (4%)
  other arithmetic  9.33 us (3%)
    all_to_all x2, waiting for transfers between devices, forward_move(): return lax.all_to_all(x, 'z', 2, 2, tiled=True)  75.4 us
    all_to_all x1, waiting for transfers between devices, backward_move(): x = lax.all_to_all(x, 'z', 2, 2, tiled=True)  57.9 us
    ppermute x6, waiting for transfers between devices, swap_half(): got = lax.ppermute(go, axis_name, SWAP)  55.4 us
    all_to_all x2, starting transfers between devices, forward_move(): return lax.all_to_all(x, 'z', 2, 2, tiled=True)  27.9 us
    ppermute x6, starting transfers between devices, swap_half(): got = lax.ppermute(go, axis_name, SWAP)  18.2 us
    concatenate x5, local copies, waits for them, and re-layouts, swap_half(): return jnp.concatenate([stay, got], dim)  7.72 us
    reduce_scatter x1, waiting for transfers between devices, body(): lax.psum_scatter(lax.dot_general(grads_in, hidden, (((0,), (0,)), ((), ()...  7.49 us
  transfers between devices with their start and end apart: 11, of which 10 were waited for; matrix products, arithmetic and copies ran while one was open for 13% of the time, Pallas kernels for 0%

profile of v2, /device:TPU:6, one launch (start us, length us, event | category | flops | bytes accessed | tf_op | source)
XLA Modules:
  0.0 326.9 jit_solution(17049731739238319428)
XLA Ops:
  7.2 2.5 pad_maximum_fusion.3
  10.2 0.6 reduce-window.6
  12.1 0.5 fusion.5
  12.7 0.3 slice.68
  13.0 0.4 copy.68
  13.4 1.9 collective-permute-start
  15.4 0.3 slice.66
  15.7 1.7 collective-permute-done
  17.4 0.4 copy_dynamic-update-slice_fusion.1
  17.8 0.2 fusion.38
  18.1 0.4 copy.70
  18.5 3.5 %collective-permute-start.1 = (bf16[2,1,16,5,2048]{4,2,3,1,0:T(8,128)(2,1)S(1)}, bf16[2,1,16,5,2048]{4,2,3,1,0:T(8,128)(2,1)S(1)}, u32[]{:S(2)}, u32[]{:S(2)}) collective-permute-start(bf16[2,1,16,5,2048]{4,2,3,1,0:T(8,128)(2,1)S(1)} %copy.70), channel_id=1, source_target_pairs={{0,32},{32,0},{1,33},{33,1},{2,34},{34,2},{3,35},{35,3},{4,36},{36... | collective-permute-start | bytes 1966088 | tf_op jit(solution)/shard_map/ppermute | solution.py:17
  22.0 16.1 %collective-permute-done.1 = bf16[2,1,16,5,2048]{4,2,3,1,0:T(8,128)(2,1)S(1)} collective-permute-done((bf16[2,1,16,5,2048]{4,2,3,1,0:T(8,128)(2,1)S(1)}, bf16[2,1,16,5,2048]{4,2,3,1,0:T(8,128)(2,1)S(1)}, u32[]{:S(2)}, u32[]{:S(2)}) %collective-permute-start.1) | collective-permute-done | bytes 655392 | tf_op jit(solution)/shard_map/ppermute | solution.py:17
  38.1 0.4 copy.71
  38.5 0.5 pad_maximum_fusion
  38.9 2.6 copy.72
  41.6 18.2 %all-to-all-start = ((bf16[2,2,16,5,2048]{4,1,3,0,2:T(2,128)(2,1)}), bf16[2,2,16,5,2048]{4,1,3,0,2:T(2,128)(2,1)S(1)}, u32[]{:S(2)}, u32[]{:S(2)}) async-start(bf16[2,2,16,5,2048]{4,1,3,0,2:T(2,128)(2,1)} %copy.72), calls=%async_computation | async-start | bytes 2621440 | tf_op jit(solution)/shard_map/all_to_all | solution.py:24
  59.8 0.5 convolution_convert_fusion.1
  60.3 1.0 fusion.42
  61.3 1.3 slice.75
  62.6 1.3 copy.74
  63.9 1.9 collective-permute-start.2
  65.8 0.3 slice.73
  66.2 2.1 collective-permute-done.2
  68.2 1.5 copy_dynamic-update-slice_fusion
  69.7 0.2 fusion.39
  69.9 0.4 copy.76
  70.4 4.6 %collective-permute-start.3 = (bf16[2,1,16,5,2048]{4,2,3,1,0:T(8,128)(2,1)S(1)}, bf16[2,1,16,5,2048]{4,2,3,1,0:T(8,128)(2,1)S(1)}, u32[]{:S(2)}, u32[]{:S(2)}) collective-permute-start(bf16[2,1,16,5,2048]{4,2,3,1,0:T(8,128)(2,1)S(1)} %copy.76), channel_id=1, source_target_pairs={{0,32},{32,0},{1,33},{33,1},{2,34},{34,2},{3,35},{35,3},{4,36},{36... | collective-permute-start | bytes 1966088 | tf_op jit(solution)/shard_map/ppermute | solution.py:17
  75.0 24.7 %collective-permute-done.3 = bf16[2,1,16,5,2048]{4,2,3,1,0:T(8,128)(2,1)S(1)} collective-permute-done((bf16[2,1,16,5,2048]{4,2,3,1,0:T(8,128)(2,1)S(1)}, bf16[2,1,16,5,2048]{4,2,3,1,0:T(8,128)(2,1)S(1)}, u32[]{:S(2)}, u32[]{:S(2)}) %collective-permute-start.3) | collective-permute-done | bytes 655392 | tf_op jit(solution)/shard_map/ppermute | solution.py:17
  99.7 0.4 copy.77
  100.1 0.5 pad_maximum_fusion.1
  100.5 2.6 copy.78
  103.2 13.9 %all-to-all-done = bf16[2,2,16,5,2048]{4,1,3,0,2:T(2,128)(2,1)S(1)} async-done(((bf16[2,2,16,5,2048]{4,1,3,0,2:T(2,128)(2,1)}), bf16[2,2,16,5,2048]{4,1,3,0,2:T(2,128)(2,1)S(1)}, u32[]{:S(2)}, u32[]{:S(2)}) %all-to-all-start) | async-done | bytes 1310752 | tf_op jit(solution)/shard_map/all_to_all | solution.py:24
  117.1 9.7 %all-to-all-start.1 = ((bf16[2,2,16,5,2048]{4,1,3,0,2:T(2,128)(2,1)}), bf16[2,2,16,5,2048]{4,1,3,0,2:T(2,128)(2,1)}, u32[]{:S(2)}, u32[]{:S(2)}) async-start(bf16[2,2,16,5,2048]{4,1,3,0,2:T(2,128)(2,1)} %copy.78), calls=%async_computation.1 | async-start | bytes 2621440 | tf_op jit(solution)/shard_map/all_to_all | solution.py:24
  126.8 0.6 copy.73
  127.5 0.6 reshape.132
  128.1 61.5 %all-to-all-done.1 = bf16[2,2,16,5,2048]{4,1,3,0,2:T(2,128)(2,1)} async-done(((bf16[2,2,16,5,2048]{4,1,3,0,2:T(2,128)(2,1)}), bf16[2,2,16,5,2048]{4,1,3,0,2:T(2,128)(2,1)}, u32[]{:S(2)}, u32[]{:S(2)}) %all-to-all-start.1) | async-done | bytes 1310752 | tf_op jit(solution)/shard_map/all_to_all | solution.py:24
  189.5 2.0 copy.79
  191.5 1.4 reshape.133
  192.9 3.6 %fusion.3 = f32[320,768]{1,0:T(8,128)S(1)} fusion(bf16[320,2048]{1,0:T(8,128)(2,1)} %reshape.133, bf16[3,2048,768]{2,1,0:T(8,128)(2,1)} %all-gather.2.cloned.1.call-done), kind=kOutput, calls=%fused_computation.9 | convolution fusion | flops 1006632960 | bytes 5439488 | tf_op jit(solution)/shard_map/dot_general | solution.py:66
  196.6 4.2 %fusion.1 = f32[320,768]{1,0:T(8,128)S(1)} fusion(bf16[320,2048]{1,0:T(8,128)(2,1)S(1)} %copy-done.2, bf16[3,2048,768]{2,1,0:T(8,128)(2,1)} %all-gather.2.cloned.1.call-done), kind=kOutput, calls=%fused_computation.7 | convolution fusion | flops 1006632960 | bytes 5439488 | tf_op jit(solution)/shard_map/dot_general | solution.py:67
  200.8 1.2 fusion
  202.0 1.4 fusion.2
  203.3 2.3 fusion.4
  205.6 2.4 reshape.134
  208.0 2.6 copy.80
  210.6 6.2 %all-to-all-start.2 = ((bf16[2,2,16,5,2048]{4,1,3,0,2:T(2,128)(2,1)}), bf16[2,2,16,5,2048]{4,1,3,0,2:T(2,128)(2,1)S(1)}, u32[]{:S(2)}, u32[]{:S(2)}) async-start(bf16[2,2,16,5,2048]{4,1,3,0,2:T(2,128)(2,1)} %copy.80), calls=%async_computation.2 | async-start | bytes 2621440 | tf_op jit(solution)/shard_map/all_to_all | solution.py:28
  216.8 0.3 reduce-scatter.2.cloned.1.call-start
  217.1 5.1 %convolution_convert_fusion = bf16[2048,768]{1,0:T(8,128)(2,1)} fusion(bf16[320,2048]{1,0:T(8,128)(2,1)S(1)} %reshape.132, f32[320,768]{1,0:T(8,128)} %copy-done.8, f32[320,768]{1,0:T(8,128)} %copy-done.7), kind=kOutput, calls=%fused_computation | convolution fusion | flops 1009680384 | bytes 6422528 | tf_op jit(solution)/shard_map/dot_general | solution.py:89
  222.2 57.9 %all-to-all-done.2 = bf16[2,2,16,5,2048]{4,1,3,0,2:T(2,128)(2,1)S(1)} async-done(((bf16[2,2,16,5,2048]{4,1,3,0,2:T(2,128)(2,1)}), bf16[2,2,16,5,2048]{4,1,3,0,2:T(2,128)(2,1)S(1)}, u32[]{:S(2)}, u32[]{:S(2)}) %all-to-all-start.2) | async-done | bytes 1310752 | tf_op jit(solution)/shard_map/all_to_all | solution.py:28
  280.1 2.8 fusion.40
  282.9 0.7 copy.81
  283.6 4.4 %collective-permute-start.4 = (bf16[2,1,16,5,2048]{4,2,3,1,0:T(8,128)(2,1)S(1)}, bf16[2,1,16,5,2048]{4,2,3,1,0:T(8,128)(2,1)S(1)}, u32[]{:S(2)}, u32[]{:S(2)}) collective-permute-start(bf16[2,1,16,5,2048]{4,2,3,1,0:T(8,128)(2,1)S(1)} %copy.81), channel_id=1, source_target_pairs={{0,32},{32,0},{1,33},{33,1},{2,34},{34,2},{3,35},{35,3},{4,36},{36... | collective-permute-start | bytes 1966088 | tf_op jit(solution)/shard_map/ppermute | solution.py:17
  288.1 8.8 %collective-permute-done.4 = bf16[2,1,16,5,2048]{4,2,3,1,0:T(8,128)(2,1)S(1)} collective-permute-done((bf16[2,1,16,5,2048]{4,2,3,1,0:T(8,128)(2,1)S(1)}, bf16[2,1,16,5,2048]{4,2,3,1,0:T(8,128)(2,1)S(1)}, u32[]{:S(2)}, u32[]{:S(2)}) %collective-permute-start.4) | collective-permute-done | bytes 655392 | tf_op jit(solution)/shard_map/ppermute | solution.py:17
  296.8 1.4 copy.82
  298.2 3.0 fusion.7
  301.4 1.9 collective-permute-start.5
  303.3 2.1 collective-permute-done.5
  305.4 0.7 copy.84
  306.1 1.8 pad_maximum_fusion.2
  307.9 0.6 copy.85
  308.5 1.4 reshape.135
  309.9 2.6 convolution_convert_fusion.2
  312.5 7.5 %reduce-scatter.2.cloned.1.call-done = bf16[256,768]{1,0:T(8,128)(2,1)} async-done(((bf16[2048,768]{1,0:T(8,128)(2,1)}), bf16[256,768]{1,0:T(8,128)(2,1)}) %reduce-scatter.2.cloned.1.call-update) | async-done | bytes 393232 | tf_op jit(solution)/shard_map/reduce_scatter | solution.py:88
  (44 shorter events, 2.2 us)
Async XLA Ops:
  7.2 5.0 %copy-start = (bf16[128,2048]{1,0:T(8,128)(2,1)S(1)}, bf16[128,2048]{1,0:T(8,128)(2,1)}, u32[]{:S(2)}) copy-start(bf16[128,2048]{1,0:T(8,128)(2,1)} %param.8) | copy-start | bytes 1572868
  7.2 2.6 copy-start.4
  7.2 4.4 %copy-start.5 = (f32[128,2]{0,1:T(2,128)S(1)}, f32[128,2]{0,1:T(2,128)}, u32[]{:S(2)}) copy-start(f32[128,2]{0,1:T(2,128)} %param.9) | copy-start | bytes 3076
  7.2 185.7 %all-gather.2.cloned.1.call-start = ((), (), s32[]{:S(2)}) async-start(), calls=%async_computation.4 | async-start | bytes 10616832 | tf_op jit(solution)/shard_map/all_gather | solution.py:40
  13.4 4.0 %collective-permute-start = (bf16[1,2,16,5,2048]{4,2,3,1,0:T(8,128)(2,1)S(1)}, bf16[1,2,16,5,2048]{4,2,3,1,0:T(8,128)(2,1)S(1)}, u32[]{:S(2)}, u32[]{:S(2)}) collective-permute-start(bf16[1,2,16,5,2048]{4,2,3,1,0:T(8,128)(2,1)S(1)} %copy.68), channel_id=1, source_target_pairs={{0,1},{1,0},{2,3},{3,2},{4,5},{5,4},{6,7},{7,6},{8,9},{9,8},{10,11... | collective-permute-start | bytes 1966088 | tf_op jit(solution)/shard_map/ppermute | solution.py:17
  18.5 19.6 %collective-permute-start.1 = (bf16[2,1,16,5,2048]{4,2,3,1,0:T(8,128)(2,1)S(1)}, bf16[2,1,16,5,2048]{4,2,3,1,0:T(8,128)(2,1)S(1)}, u32[]{:S(2)}, u32[]{:S(2)}) collective-permute-start(bf16[2,1,16,5,2048]{4,2,3,1,0:T(8,128)(2,1)S(1)} %copy.70), channel_id=1, source_target_pairs={{0,32},{32,0},{1,33},{33,1},{2,34},{34,2},{3,35},{35,3},{4,36},{36... | collective-permute-start | bytes 1966088 | tf_op jit(solution)/shard_map/ppermute | solution.py:17
  41.6 18.2 %copy-start.3 = (bf16[128,2048]{1,0:T(8,128)(2,1)S(1)}, bf16[128,2048]{1,0:T(8,128)(2,1)}, u32[]{:S(2)}) copy-start(bf16[128,2048]{1,0:T(8,128)(2,1)} %param.7) | copy-start | bytes 1572868
  41.6 75.5 %all-to-all-start = ((bf16[2,2,16,5,2048]{4,1,3,0,2:T(2,128)(2,1)}), bf16[2,2,16,5,2048]{4,1,3,0,2:T(2,128)(2,1)S(1)}, u32[]{:S(2)}, u32[]{:S(2)}) async-start(bf16[2,2,16,5,2048]{4,1,3,0,2:T(2,128)(2,1)} %copy.72), calls=%async_computation | async-start | bytes 2621440 | tf_op jit(solution)/shard_map/all_to_all | solution.py:24
  63.9 4.3 %collective-permute-start.2 = (bf16[1,2,16,5,2048]{4,2,3,1,0:T(8,128)(2,1)}, bf16[1,2,16,5,2048]{4,2,3,1,0:T(8,128)(2,1)}, u32[]{:S(2)}, u32[]{:S(2)}) collective-permute-start(bf16[1,2,16,5,2048]{4,2,3,1,0:T(8,128)(2,1)} %copy.74), channel_id=1, source_target_pairs={{0,1},{1,0},{2,3},{3,2},{4,5},{5,4},{6,7},{7,6},{8,9},{9,8},{10,11... | collective-permute-start | bytes 1966088 | tf_op jit(solution)/shard_map/ppermute | solution.py:17
  70.4 29.3 %collective-permute-start.3 = (bf16[2,1,16,5,2048]{4,2,3,1,0:T(8,128)(2,1)S(1)}, bf16[2,1,16,5,2048]{4,2,3,1,0:T(8,128)(2,1)S(1)}, u32[]{:S(2)}, u32[]{:S(2)}) collective-permute-start(bf16[2,1,16,5,2048]{4,2,3,1,0:T(8,128)(2,1)S(1)} %copy.76), channel_id=1, source_target_pairs={{0,32},{32,0},{1,33},{33,1},{2,34},{34,2},{3,35},{35,3},{4,36},{36... | collective-permute-start | bytes 1966088 | tf_op jit(solution)/shard_map/ppermute | solution.py:17
  117.1 72.4 %all-to-all-start.1 = ((bf16[2,2,16,5,2048]{4,1,3,0,2:T(2,128)(2,1)}), bf16[2,2,16,5,2048]{4,1,3,0,2:T(2,128)(2,1)}, u32[]{:S(2)}, u32[]{:S(2)}) async-start(bf16[2,2,16,5,2048]{4,1,3,0,2:T(2,128)(2,1)} %copy.78), calls=%async_computation.1 | async-start | bytes 2621440 | tf_op jit(solution)/shard_map/all_to_all | solution.py:24
  192.9 3.6 %copy-start.2 = (bf16[320,2048]{1,0:T(8,128)(2,1)S(1)}, bf16[320,2048]{1,0:T(8,128)(2,1)}, u32[]{:S(2)}) copy-start(bf16[320,2048]{1,0:T(8,128)(2,1)} %reshape.133) | copy-start | bytes 3932164
  192.9 7.8 %copy-start.6 = (bf16[3,2048,768]{2,1,0:T(8,128)(2,1)S(1)}, bf16[3,2048,768]{2,1,0:T(8,128)(2,1)}, u32[]{:S(2)}) copy-start(bf16[3,2048,768]{2,1,0:T(8,128)(2,1)} %all-gather.2.cloned.1.call-done) | copy-start | bytes 28311556
  196.6 6.8 %copy-start.7 = (f32[320,768]{1,0:T(8,128)}, f32[320,768]{1,0:T(8,128)S(1)}, u32[]{:S(2)}) copy-start(f32[320,768]{1,0:T(8,128)S(1)} %fusion.3) | copy-start | bytes 2949124
  200.8 1.2 copy-start.8
  210.6 69.4 %all-to-all-start.2 = ((bf16[2,2,16,5,2048]{4,1,3,0,2:T(2,128)(2,1)}), bf16[2,2,16,5,2048]{4,1,3,0,2:T(2,128)(2,1)S(1)}, u32[]{:S(2)}, u32[]{:S(2)}) async-start(bf16[2,2,16,5,2048]{4,1,3,0,2:T(2,128)(2,1)} %copy.80), calls=%async_computation.2 | async-start | bytes 2621440 | tf_op jit(solution)/shard_map/all_to_all | solution.py:28
  216.8 103.2 %reduce-scatter.2.cloned.1.call-start = ((), (), s32[]{:S(2)}) async-start(), calls=%async_computation.5 | async-start | bytes 3538944 | tf_op jit(solution)/shard_map/reduce_scatter | solution.py:88
  283.6 13.2 %collective-permute-start.4 = (bf16[2,1,16,5,2048]{4,2,3,1,0:T(8,128)(2,1)S(1)}, bf16[2,1,16,5,2048]{4,2,3,1,0:T(8,128)(2,1)S(1)}, u32[]{:S(2)}, u32[]{:S(2)}) collective-permute-start(bf16[2,1,16,5,2048]{4,2,3,1,0:T(8,128)(2,1)S(1)} %copy.81), channel_id=1, source_target_pairs={{0,32},{32,0},{1,33},{33,1},{2,34},{34,2},{3,35},{35,3},{4,36},{36... | collective-permute-start | bytes 1966088 | tf_op jit(solution)/shard_map/ppermute | solution.py:17
  301.4 4.0 %collective-permute-start.5 = (bf16[1,2,16,5,2048]{4,2,3,1,0:T(8,128)(2,1)S(1)}, bf16[1,2,16,5,2048]{4,2,3,1,0:T(8,128)(2,1)S(1)}, u32[]{:S(2)}, u32[]{:S(2)}) collective-permute-start(bf16[1,2,16,5,2048]{4,2,3,1,0:T(8,128)(2,1)S(1)} %copy.83), channel_id=1, source_target_pairs={{0,1},{1,0},{2,3},{3,2},{4,5},{5,4},{6,7},{7,6},{8,9},{9,8},{10,11... | collective-permute-start | bytes 1966088 | tf_op jit(solution)/shard_map/ppermute | solution.py:17
  307.9 12.2 %copy-start.1 = (bf16[128,2048]{1,0:T(8,128)(2,1)S(1)}, bf16[128,2048]{1,0:T(8,128)(2,1)}, u32[]{:S(2)}) copy-start(bf16[128,2048]{1,0:T(8,128)(2,1)} %param.8) | copy-start | bytes 1572868
Sparse Core Ops, SparseCore 0:
  11.2 149.9 all-gather.1
  223.0 96.9 reduce-scatter.1
